TPU v7x, 256 devices: a whole 4x4x8 slice. The times are simulated.
256 devices in a mesh: stream: 8 (over z), span: 32 (over y, x, core).
Axes of the slice: x: 4, y: 4, z: 8, core: 2. Of those that a mesh axis runs over, the one named last changes fastest.
Arguments:
- velocity: float32 [3, 64, 512, 1024], P(None, 'stream', 'span'), may hold values from -36 to 36
- coefficient: float32 [64, 512, 1024], P('stream', 'span'), may hold values from 0.5 to 4
- coords: float32 [3, 32768], P(None, ('stream', 'span')), may hold values from -1 to 1
- forces: float32 [3, 32768], P(None, ('stream', 'span')), may hold values from -12 to 12
- line_id: int32 [32768], P(('stream', 'span')), may hold values from 0 to 399
- line_gain: float32 [400], replicated, may hold values from 0.5 to 2
- dest_span: int32 [32768, 1], P(('stream', 'span')), may hold values from 0 to 31; in each aligned block of 128 rows (0 to 127, 128 to 255, ...) at most 8 rows name the same one
- owner_element: int32 [32768], P(('stream', 'span')), may hold values from 0 to 255
Outputs:
- pressure: float32 [64, 512, 1024], P('stream', 'span')
- residual: float32 [64, 512, 1024], P('stream', 'span')
Inputs may be any that keep to these rules, and one draw needn't show every extreme that they name: `dest_span`: of the 128 blade points of one device, at most 8 name the same span index, and in every draw some span index is named by exactly 8 of one device's points. `owner_element`: an element of the device at the point's span index in the same slab, numbered (ex * 2 + ey) * 128 + ez.
All inputs are finite; a program needn't handle non-finite values.
Results may differ from a plain program's by a relative error of at most 0.00019.
Values sent between devices are 32-bit elements; how exact they have to be, the bound alone decides.
No kernel may reach another device: no remote copies, remote signals or barrier semaphores. Data moves between devices by JAX's collectives and lax.ppermute only.
A program may use at most 64 MiB of HBM per device.

v0:
```python
import jax
import jax.numpy as jnp
from jax import lax
from jax.sharding import PartitionSpec as P

POLY = 8
ITERS = 3
kernel_width = 0.45
gll_nodes = [
    -1.0,
    -0.8717401485096066,
    -0.5917001814331423,
    -0.2092992179024789,
    0.2092992179024789,
    0.5917001814331423,
    0.8717401485096066,
    1.0,
]


def with_halo(x, sides, width):
    for axis, dim in sides:
        size, length = (lax.axis_size(axis), x.shape[dim])
        up = [(i, (i + 1) % size) for i in range(size - 1)]
        down = [(j, i) for i, j in up]
        last = lax.slice_in_dim(x, length - width, length, axis=dim)
        first = lax.slice_in_dim(x, 0, width, axis=dim)
        before = lax.ppermute(last, axis, up)
        after = lax.ppermute(first, axis, down)
        x = jnp.concatenate([before, x, after], axis=dim)
    return x


def legendre_value(point, degree):
    previous = 1.0
    current = point
    for order in range(1, degree):
        following = ((2 * order + 1) * point * current - order * previous) / (order + 1)
        previous = current
        current = following
    return current


def gll_tables():
    degree = POLY - 1
    values = [legendre_value(point, degree) for point in gll_nodes]
    weights = [2.0 / (degree * (degree + 1) * value * value) for value in values]
    diffmat = []
    for row_at in range(POLY):
        row_list = []
        for col_at in range(POLY):
            if row_at != col_at:
                row_list.append(
                    values[row_at] / (values[col_at] * (gll_nodes[row_at] - gll_nodes[col_at]))
                )
            elif row_at == 0:
                row_list.append(-degree * (degree + 1) / 4.0)
            elif row_at == degree:
                row_list.append(degree * (degree + 1) / 4.0)
            else:
                row_list.append(0.0)
        diffmat.append(row_list)
    return (
        jnp.asarray(gll_nodes, dtype=jnp.float32),
        jnp.asarray(weights, dtype=jnp.float32),
        jnp.asarray(diffmat, dtype=jnp.float32),
    )


def derive(grid_field, diffmat, axis_at, flipped):
    matrix = diffmat.T if flipped else diffmat
    extent0, extent1, extent2 = grid_field.shape
    highest = lax.Precision.HIGHEST
    if axis_at == 0:
        blocks = grid_field.reshape(extent0 // POLY, POLY, extent1, extent2)
        result = jnp.einsum("ia,xayz->xiyz", matrix, blocks, precision=highest)
    elif axis_at == 1:
        blocks = grid_field.reshape(extent0, extent1 // POLY, POLY, extent2)
        result = jnp.einsum("ib,xybz->xyiz", matrix, blocks, precision=highest)
    else:
        block_width = 128
        tiled_matrix = jnp.kron(jnp.eye(block_width // POLY, dtype=jnp.float32), matrix)
        blocks = grid_field.reshape(extent0, extent1, extent2 // block_width, block_width)
        result = jnp.einsum("xyzc,ic->xyzi", blocks, tiled_matrix, precision=highest)
    return result.reshape(grid_field.shape)


def face_masks(extent):
    node = lax.iota(jnp.int32, extent) % POLY
    return (node == 0, node == POLY - 1)


def assemble(grid_field):
    extent0, extent1, extent2 = grid_field.shape
    first0, last0 = face_masks(extent0)
    first1, last1 = face_masks(extent1)
    first2, last2 = face_masks(extent2)
    first0, last0 = (first0[:, None, None], last0[:, None, None])
    first1, last1 = (first1[None, :, None], last1[None, :, None])
    first2, last2 = (first2[None, None, :], last2[None, None, :])
    nothing = jnp.zeros_like(grid_field)
    padded = with_halo(grid_field, (("stream", 0),), 1)
    running = (
        grid_field + jnp.where(first0, padded[:-2], nothing) + jnp.where(last0, padded[2:], nothing)
    )
    padded = with_halo(running, (("span", 1),), 1)
    running = (
        running
        + jnp.where(first1, padded[:, :-2], nothing)
        + jnp.where(last1, padded[:, 2:], nothing)
    )
    before = jnp.pad(running, ((0, 0), (0, 0), (1, 0)))[:, :, :-1]
    after = jnp.pad(running, ((0, 0), (0, 0), (0, 1)))[:, :, 1:]
    return running + jnp.where(first2, before, nothing) + jnp.where(last2, after, nothing)


def inverse_multiplicity(extent, offset, whole):
    node = lax.iota(jnp.int32, extent) % POLY
    position = offset + lax.iota(jnp.int32, extent)
    inner_face = (node == 0) & (position > 0) | (node == POLY - 1) & (position < whole - 1)
    return jnp.where(inner_face, 0.5, 1.0).astype(jnp.float32)


def apply_operator(grid_field, weight3, metric, diffmat):
    running = weight3 * grid_field
    for axis_at in range(3):
        running = running + derive(
            metric * derive(grid_field, diffmat, axis_at, False), diffmat, axis_at, True
        )
    return assemble(running)


def spread_points(arrived, abscissa, extent0, extent1, extent2):
    slots = arrived.shape[0]
    elems_x, elems_y, elems_z = (extent0 // POLY, extent1 // POLY, extent2 // POLY)
    kernels = []
    for dimension in range(3):
        kernels.append(
            jnp.exp(
                -(((abscissa[None, :] - arrived[:, dimension : dimension + 1]) / kernel_width) ** 2)
            )
        )
    kernel3 = (
        kernels[0][:, :, None, None] * kernels[1][:, None, :, None] * kernels[2][:, None, None, :]
    )
    contrib = (arrived[:, 3:6][:, :, None, None, None] * kernel3[:, None]).reshape(
        slots, 3 * POLY**3
    )
    element_codes = lax.iota(jnp.float32, elems_x * elems_y * elems_z) + 1.0
    onehot = (arrived[:, 6][:, None] == element_codes[None, :]).astype(jnp.float32)
    per_elem = jnp.dot(
        onehot.T, contrib, precision=lax.Precision.HIGHEST, preferred_element_type=jnp.float32
    )
    per_elem = per_elem.reshape(elems_x, elems_y, elems_z, 3, POLY, POLY, POLY)
    return per_elem.transpose(3, 0, 4, 1, 5, 2, 6).reshape(3, extent0, extent1, extent2)


def project_points(coords, forces, line_id, line_gain, dest_span, owner_element, abscissa, extents):
    points_dev = coords.shape[1]
    spans = lax.axis_size("span")
    capacity = max(2, 2 * points_dev // spans)
    table_ids = lax.iota(jnp.int32, line_gain.shape[0])
    gains = jnp.sum(
        jnp.where(line_id[:, None] == table_ids[None, :], line_gain[None, :], 0.0), axis=1
    )
    scaled = forces * gains[None, :]
    target = dest_span[:, 0]
    owner_code = (owner_element + 1).astype(jnp.float32)
    payload = jnp.concatenate(
        [coords, scaled, owner_code[None, :], target.astype(jnp.float32)[None, :]], axis=0
    ).T
    onehot_dest = (target[:, None] == lax.iota(jnp.int32, spans)[None, :]).astype(jnp.int32)
    ranks = jnp.sum((jnp.cumsum(onehot_dest, axis=0) - 1) * onehot_dest, axis=1)
    slot_at = target * capacity + ranks
    outgoing = jnp.zeros((spans * capacity, 8), jnp.float32).at[slot_at].set(payload)
    outgoing = outgoing.reshape(spans, capacity, 8)
    arrived = lax.all_to_all(outgoing, "span", split_axis=0, concat_axis=0, tiled=True).reshape(
        spans * capacity, 8
    )
    return spread_points(arrived, abscissa, extents[0], extents[1], extents[2])


def on_device(velocity, coefficient, coords, forces, line_id, line_gain, dest_span, owner_element):
    abscissa, weights, diffmat = gll_tables()
    extent0, extent1, extent2 = coefficient.shape
    tile_zero = jnp.tile(weights, extent0 // POLY)
    tile_one = jnp.tile(weights, extent1 // POLY)
    tile_two = jnp.tile(weights, extent2 // POLY)
    weight3 = tile_zero[:, None, None] * tile_one[None, :, None] * tile_two[None, None, :]
    metric = weight3 * coefficient
    inv_zero = inverse_multiplicity(
        extent0, lax.axis_index("stream") * extent0, extent0 * lax.axis_size("stream")
    )
    inv_one = inverse_multiplicity(
        extent1, lax.axis_index("span") * extent1, extent1 * lax.axis_size("span")
    )
    inv_two = inverse_multiplicity(extent2, 0, extent2)
    inv_mult = inv_zero[:, None, None] * inv_one[None, :, None] * inv_two[None, None, :]
    forcing = project_points(
        coords,
        forces,
        line_id,
        line_gain,
        dest_span,
        owner_element,
        abscissa,
        (extent0, extent1, extent2),
    )
    running = derive(weight3 * (velocity[0] + forcing[0]), diffmat, 0, True)
    running = running + derive(weight3 * (velocity[1] + forcing[1]), diffmat, 1, True)
    running = running + derive(weight3 * (velocity[2] + forcing[2]), diffmat, 2, True)
    rhs = assemble(running)

    def weighted(first_vec, second_vec):
        return jnp.sum(first_vec * second_vec * inv_mult)

    def squares(residual):
        return lax.psum(weighted(residual, residual), ("stream", "span"))

    pressure = jnp.zeros_like(rhs)
    residual = rhs
    direction = rhs
    norm_now = squares(residual)
    for iteration in range(ITERS):
        applied = apply_operator(direction, weight3, metric, diffmat)
        step_len = norm_now / lax.psum(weighted(direction, applied), ("stream", "span"))
        pressure = pressure + step_len * direction
        residual = residual - step_len * applied
        norm_next = squares(residual)
        direction = residual + norm_next / norm_now * direction
        norm_now = norm_next
    return (pressure, residual)


def solution(mesh):
    return jax.shard_map(
        on_device,
        mesh=mesh,
        in_specs=(
            P(None, "stream", "span", None),
            P("stream", "span", None),
            P(None, ("stream", "span")),
            P(None, ("stream", "span")),
            P(("stream", "span")),
            P(),
            P(("stream", "span"), None),
            P(("stream", "span")),
        ),
        out_specs=(P("stream", "span", None), P("stream", "span", None)),
        check_vma=False,
    )
```

profile of v0, /device:TPU:1, one launch (start us, length us, event | category | flops | bytes accessed | tf_op | source)
XLA Modules:
  0.0 554.8 jit_solution(15528119805396378433)
XLA Ops:
  7.8 8.6 %all-to-all-start = ((f32[32,8,8]{1,2,0:T(8,128)}), f32[32,8,8]{1,2,0:T(8,128)S(1)}, u32[]{:S(2)}, u32[]{:S(2)}) async-start(f32[32,8,8]{1,2,0:T(8,128)} %copy.228), calls=%async_computation | async-start | bytes 262144 | tf_op jit(solution)/shard_map/all_to_all | solution.py:177
  20.2 3.7 all-to-all-done
  25.5 4.6 copy.230
  30.0 6.9 %squeeze.15 = f32[1,8,16,1024]{3,2,1,0:T(8,128)S(1)} reshape(f32[1,1,8,2,8,128,8]{6,5,4,3,2,1,0:T(8,128)} %copy.230) | data formatting | bytes 1048576 | tf_op jit(solution)/shard_map/squeeze | solution.py:209
  36.9 4.6 copy.234
  41.5 6.9 %squeeze.18 = f32[1,8,16,1024]{3,2,1,0:T(8,128)S(1)} reshape(f32[1,1,8,2,8,128,8]{6,5,4,3,2,1,0:T(8,128)} %copy.234) | data formatting | bytes 1048576 | tf_op jit(solution)/shard_map/squeeze | solution.py:211
  49.8 4.6 copy.232
  54.4 6.9 %squeeze.17 = f32[8,2,8,1024]{3,2,1,0:T(8,128)S(1)} reshape(f32[1,1,8,2,8,128,8]{6,5,4,3,2,1,0:T(8,128)} %copy.232) | data formatting | bytes 1048576 | tf_op jit(solution)/shard_map/squeeze | solution.py:210
  65.2 3.5 collective-permute-start
  70.1 3.9 collective-permute-done.1
  74.2 3.8 collective-permute-start.2
  89.6 3.5 collective-permute-start.4
  94.5 4.9 collective-permute-done.5
  109.6 80.7 %all-reduce.8 = (f32[]{:T(128)}, f32[]{:T(128)}) all-reduce(f32[]{:T(128)} %get-tuple-element.15, f32[]{:T(128)} %get-tuple-element.14), channel_id=1, replica_groups=mesh['stream'=8,'span'=32] {'stream','span'}, use_global_device_ids=true, to_apply=%region_5.6 | all-reduce | flops 2 | bytes 16 | tf_op jit(solution)/shard_map/psum | solution.py:218
  192.6 73.5 %psum.44 = f32[]{:T(128)} all-reduce(f32[]{:T(128)} %fusion.47), channel_id=1, replica_groups=mesh['stream'=8,'span'=32] {'stream','span'}, use_global_device_ids=true, to_apply=%region_9.10 | all-reduce | flops 1 | bytes 8 | tf_op jit(solution)/shard_map/psum | solution.py:218
  273.6 3.7 collective-permute-start.8
  278.6 3.7 collective-permute-done.9
  282.5 4.9 collective-permute-start.10
  293.9 76.7 %psum.45 = f32[]{:T(128)} all-reduce(f32[]{:T(128)} %get-tuple-element.22), channel_id=1, replica_groups=mesh['stream'=8,'span'=32] {'stream','span'}, use_global_device_ids=true, to_apply=%region_11.12 | all-reduce | flops 1 | bytes 8 | tf_op jit(solution)/shard_map/psum | solution.py:226
  372.9 73.5 %psum.46 = f32[]{:T(128)} all-reduce(f32[]{:T(128)} %get-tuple-element.20), channel_id=1, replica_groups=mesh['stream'=8,'span'=32] {'stream','span'}, use_global_device_ids=true, to_apply=%region_13.14 | all-reduce | flops 1 | bytes 8 | tf_op jit(solution)/shard_map/psum | solution.py:218
  453.6 3.7 collective-permute-start.12
  458.6 3.7 collective-permute-done.13
  462.6 5.0 collective-permute-start.14
  473.9 76.7 %psum.47 = f32[]{:T(128)} all-reduce(f32[]{:T(128)} %get-tuple-element.18), channel_id=1, replica_groups=mesh['stream'=8,'span'=32] {'stream','span'}, use_global_device_ids=true, to_apply=%region_15.16 | all-reduce | flops 1 | bytes 8 | tf_op jit(solution)/shard_map/psum | solution.py:226
  (131 shorter events, 74.4 us)
Async XLA Ops:
  1.3 18.3 %copy-start.3 = (f32[8]{0:T(128)S(1)}, f32[8]{0:T(128)}, u32[]{:S(2)}) copy-start(f32[8]{0:T(128)} %constant.131.clone) | copy-start | bytes 100
  7.8 16.2 %all-to-all-start = ((f32[32,8,8]{1,2,0:T(8,128)}), f32[32,8,8]{1,2,0:T(8,128)S(1)}, u32[]{:S(2)}, u32[]{:S(2)}) async-start(f32[32,8,8]{1,2,0:T(8,128)} %copy.228), calls=%async_computation | async-start | bytes 262144 | tf_op jit(solution)/shard_map/all_to_all | solution.py:177
  18.7 5.4 copy-start.4
  54.4 6.9 %copy-start.2 = (f32[8,8,1,1]{0,1,3,2:T(8,128)S(1)}, f32[8,8,1,1]{0,1,3,2:T(8,128)}, u32[]{:S(2)}) copy-start(f32[8,8,1,1]{0,1,3,2:T(8,128)} %constant.158) | copy-start | bytes 772
  61.3 2.9 copy-start.1
  65.2 4.9 collective-permute-start
  68.8 5.2 collective-permute-start.1
  74.2 6.8 %collective-permute-start.2 = (f32[8,1,1024]{2,0,1:T(8,128)S(1)}, f32[8,1,1024]{2,0,1:T(8,128)S(1)}, u32[]{:S(2)}, u32[]{:S(2)}) collective-permute-start(f32[8,1,1024]{2,0,1:T(8,128)S(1)} %get-tuple-element.42), channel_id=1, source_target_pairs={{0,1},{1,2},{2,3},{3,4},{4,5},{5,6},{6,7},{7,8},{8,9},{9,10},{10,1... | collective-permute-start | bytes 98312 | tf_op jit(solution)/shard_map/ppermute | solution.py:28
  78.0 5.2 collective-permute-start.3
  83.4 1.6 copy-start
  89.6 4.9 collective-permute-start.4
  93.1 6.3 %collective-permute-start.5 = (f32[1,16,1024]{2,0,1:T(1,128)S(1)}, f32[1,16,1024]{2,0,1:T(1,128)S(1)}, u32[]{:S(2)}, u32[]{:S(2)}) collective-permute-start(f32[1,16,1024]{2,0,1:T(1,128)S(1)} %get-tuple-element.41), channel_id=1, source_target_pairs={{32,0},{64,32},{96,64},{128,96},{160,128},{192,160},{224,192},{33,... | collective-permute-start | bytes 196616 | tf_op jit(solution)/shard_map/ppermute | solution.py:29
  99.7 5.3 collective-permute-start.6
  103.0 5.2 collective-permute-start.7
  273.6 5.0 collective-permute-start.8
  277.3 5.0 collective-permute-start.9
  282.5 6.9 %collective-permute-start.10 = (f32[8,1,1024]{2,0,1:T(8,128)S(1)}, f32[8,1,1024]{2,0,1:T(8,128)S(1)}, u32[]{:S(2)}, u32[]{:S(2)}) collective-permute-start(f32[8,1,1024]{2,0,1:T(8,128)S(1)} %get-tuple-element.34), channel_id=1, source_target_pairs={{0,1},{1,2},{2,3},{3,4},{4,5},{5,6},{6,7},{7,8},{8,9},{9,10},{10,1... | collective-permute-start | bytes 98312 | tf_op jit(solution)/shard_map/ppermute | solution.py:28
  287.5 5.2 collective-permute-start.11
  453.6 5.0 collective-permute-start.12
  457.3 5.0 collective-permute-start.13
  462.6 6.9 %collective-permute-start.14 = (f32[8,1,1024]{2,0,1:T(8,128)S(1)}, f32[8,1,1024]{2,0,1:T(8,128)S(1)}, u32[]{:S(2)}, u32[]{:S(2)}) collective-permute-start(f32[8,1,1024]{2,0,1:T(8,128)S(1)} %get-tuple-element.30), channel_id=1, source_target_pairs={{0,1},{1,2},{2,3},{3,4},{4,5},{5,6},{6,7},{7,8},{8,9},{9,10},{10,1... | collective-permute-start | bytes 98312 | tf_op jit(solution)/shard_map/ppermute | solution.py:28
  467.5 5.2 collective-permute-start.15
where the time goes:
time: 565 us; the launch traced here: 555 us
  blocking collectives  381 us (67%)
  starting transfers between devices  53.3 us (9%)
  local copies, waits for them, and re-layouts  43.2 us (8%)
  waiting for transfers between devices  32.1 us (6%)
  other arithmetic  18.4 us (3%)
  matrix products  18.4 us (3%)
  between operations  8.33 us (1%)
    psum x3, blocking collectives, squares(): return lax.psum(weighted(residual, residual), ('stream', 'span'))  228 us
    psum x2, blocking collectives, on_device(): lax.psum(weighted(direction, applied), ('stream', 'span'))  153 us
    ppermute x8, starting transfers between devices, with_halo(): before = lax.ppermute(last, axis, up)  31.4 us
    ppermute x8, waiting for transfers between devices, with_halo(): after = lax.ppermute(first, axis, down)  28.3 us
    ppermute x8, starting transfers between devices, with_halo(): after = lax.ppermute(first, axis, down)  13.3 us
  transfers between devices with their start and end apart: 17, of which 9 were waited for; matrix products, arithmetic and copies ran while one was open for 1% of the time, Pallas kernels for 0%

commit v1 on v0

--- a/solution.py
+++ b/solution.py
@@ -1,3 +1,4 @@
+import functools
 import jax
 import jax.numpy as jnp
 from jax import lax
@@ -16,6 +17,14 @@
     0.8717401485096066,
     1.0,
 ]
+
+
+def render_tasks_up(tile_in, a_name):
+    b_now = lax.all_gather(tile_in, axis_name=a_name)
+    return jnp.sum(b_now, axis=0)
+
+
+arrange_the_sections = functools.partial(render_tasks_up, a_name=("stream", "span"))
 
 
 def with_halo(x, sides, width):
@@ -215,7 +224,7 @@
         return jnp.sum(first_vec * second_vec * inv_mult)
 
     def squares(residual):
-        return lax.psum(weighted(residual, residual), ("stream", "span"))
+        return arrange_the_sections(weighted(residual, residual))
 
     pressure = jnp.zeros_like(rhs)
     residual = rhs

time: 565 us -> 569 us (level)
    psum x3 -> x0, blocking collectives: 228 us -> none  [squares(): return lax.psum(weighted(residual, residual), ('stream', 'span'))]
    unnamed x0 -> x3, blocking collectives: none -> 228 us
where the time goes in v1:
time: 569 us; the launch traced here: 559 us
  blocking collectives  381 us (67%)
  starting transfers between devices  53.4 us (9%)
  local copies, waits for them, and re-layouts  45.5 us (8%)
  waiting for transfers between devices  32.1 us (6%)
  other arithmetic  20.2 us (4%)
  matrix products  18.4 us (3%)
  between operations  8.35 us (1%)
    unnamed x3, blocking collectives  228 us
    psum x2, blocking collectives, on_device(): lax.psum(weighted(direction, applied), ('stream', 'span'))  153 us
    ppermute x8, starting transfers between devices, with_halo(): before = lax.ppermute(last, axis, up)  31.5 us
    ppermute x8, waiting for transfers between devices, with_halo(): after = lax.ppermute(first, axis, down)  28.3 us
    ppermute x8, starting transfers between devices, with_halo(): after = lax.ppermute(first, axis, down)  13.3 us
  transfers between devices with their start and end apart: 17, of which 9 were waited for; matrix products, arithmetic and copies ran while one was open for 1% of the time, Pallas kernels for 0%

profile of v1, /device:TPU:1, one launch (start us, length us, event | category | flops | bytes accessed | tf_op | source)
XLA Modules:
  0.0 559.0 jit_solution(7259559487240628648)
XLA Ops:
  7.8 8.6 %all-to-all-start = ((f32[32,8,8]{1,2,0:T(8,128)}), f32[32,8,8]{1,2,0:T(8,128)S(1)}, u32[]{:S(2)}, u32[]{:S(2)}) async-start(f32[32,8,8]{1,2,0:T(8,128)} %copy.228), calls=%async_computation | async-start | bytes 262144 | tf_op jit(solution)/shard_map/all_to_all | solution.py:186
  20.2 3.7 all-to-all-done
  25.4 4.6 copy.230
  30.0 6.9 %squeeze.15 = f32[1,8,16,1024]{3,2,1,0:T(8,128)S(1)} reshape(f32[1,1,8,2,8,128,8]{6,5,4,3,2,1,0:T(8,128)} %copy.230) | data formatting | bytes 1048576 | tf_op jit(solution)/shard_map/squeeze | solution.py:218
  36.9 4.6 copy.234
  41.5 6.9 %squeeze.18 = f32[1,8,16,1024]{3,2,1,0:T(8,128)S(1)} reshape(f32[1,1,8,2,8,128,8]{6,5,4,3,2,1,0:T(8,128)} %copy.234) | data formatting | bytes 1048576 | tf_op jit(solution)/shard_map/squeeze | solution.py:220
  49.8 4.6 copy.232
  54.4 6.9 %squeeze.17 = f32[8,2,8,1024]{3,2,1,0:T(8,128)S(1)} reshape(f32[1,1,8,2,8,128,8]{6,5,4,3,2,1,0:T(8,128)} %copy.232) | data formatting | bytes 1048576 | tf_op jit(solution)/shard_map/squeeze | solution.py:219
  65.2 3.5 collective-permute-start
  70.1 3.9 collective-permute-done.1
  74.3 3.8 collective-permute-start.2
  89.6 3.6 collective-permute-start.4
  94.5 4.9 collective-permute-done.5
  110.5 80.6 %all-reduce.11 = (f32[256]{0:T(256)S(1)}, f32[]{:T(128)}) all-reduce(f32[256]{0:T(256)S(1)} %dynamic-update-slice, f32[]{:T(128)} %get-tuple-element.14), channel_id=1, replica_groups=mesh['stream'=8,'span'=32] {'stream','span'}, use_global_device_ids=true, to_apply=%add.8 | all-reduce | flops 257 | bytes 2056
  194.8 73.5 %all-reduce.9 = f32[256]{0:T(256)S(1)} all-reduce(f32[256]{0:T(256)S(1)} %dynamic-update-slice.1), channel_id=1, replica_groups=mesh['stream'=8,'span'=32] {'stream','span'}, use_global_device_ids=true, to_apply=%add.9 | all-reduce | flops 256 | bytes 2048
  276.3 3.7 collective-permute-start.8
  281.3 3.7 collective-permute-done.9
  285.3 5.0 collective-permute-start.10
  296.7 76.7 %psum.22 = f32[]{:T(128)} all-reduce(f32[]{:T(128)} %get-tuple-element.22), channel_id=1, replica_groups=mesh['stream'=8,'span'=32] {'stream','span'}, use_global_device_ids=true, to_apply=%region_11.12 | all-reduce | flops 1 | bytes 8 | tf_op jit(solution)/shard_map/psum | solution.py:235
  376.4 73.5 %all-reduce.10 = f32[256]{0:T(256)S(1)} all-reduce(f32[256]{0:T(256)S(1)} %dynamic-update-slice.2), channel_id=1, replica_groups=mesh['stream'=8,'span'=32] {'stream','span'}, use_global_device_ids=true, to_apply=%add.10 | all-reduce | flops 256 | bytes 2048
  457.7 3.7 collective-permute-start.12
  462.7 3.7 collective-permute-done.13
  466.7 5.0 collective-permute-start.14
  478.1 76.7 %psum.23 = f32[]{:T(128)} all-reduce(f32[]{:T(128)} %get-tuple-element.18), channel_id=1, replica_groups=mesh['stream'=8,'span'=32] {'stream','span'}, use_global_device_ids=true, to_apply=%region_15.16 | all-reduce | flops 1 | bytes 8 | tf_op jit(solution)/shard_map/psum | solution.py:235
  (140 shorter events, 78.5 us)
Async XLA Ops:
  1.3 18.3 %copy-start.3 = (f32[8]{0:T(128)S(1)}, f32[8]{0:T(128)}, u32[]{:S(2)}) copy-start(f32[8]{0:T(128)} %constant.131.clone) | copy-start | bytes 100
  7.8 16.2 %all-to-all-start = ((f32[32,8,8]{1,2,0:T(8,128)}), f32[32,8,8]{1,2,0:T(8,128)S(1)}, u32[]{:S(2)}, u32[]{:S(2)}) async-start(f32[32,8,8]{1,2,0:T(8,128)} %copy.228), calls=%async_computation | async-start | bytes 262144 | tf_op jit(solution)/shard_map/all_to_all | solution.py:186
  18.7 5.4 copy-start.4
  54.4 6.9 %copy-start.2 = (f32[8,8,1,1]{0,1,3,2:T(8,128)S(1)}, f32[8,8,1,1]{0,1,3,2:T(8,128)}, u32[]{:S(2)}) copy-start(f32[8,8,1,1]{0,1,3,2:T(8,128)} %constant.170) | copy-start | bytes 772
  61.3 2.9 copy-start.1
  65.2 4.9 collective-permute-start
  68.8 5.2 collective-permute-start.1
  74.3 6.8 %collective-permute-start.2 = (f32[8,1,1024]{2,0,1:T(8,128)S(1)}, f32[8,1,1024]{2,0,1:T(8,128)S(1)}, u32[]{:S(2)}, u32[]{:S(2)}) collective-permute-start(f32[8,1,1024]{2,0,1:T(8,128)S(1)} %get-tuple-element.42), channel_id=1, source_target_pairs={{0,1},{1,2},{2,3},{3,4},{4,5},{5,6},{6,7},{7,8},{8,9},{9,10},{10,1... | collective-permute-start | bytes 98312 | tf_op jit(solution)/shard_map/ppermute | solution.py:37
  78.0 5.2 collective-permute-start.3
  83.4 1.6 copy-start
  89.6 4.9 collective-permute-start.4
  93.2 6.3 %collective-permute-start.5 = (f32[1,16,1024]{2,0,1:T(1,128)S(1)}, f32[1,16,1024]{2,0,1:T(1,128)S(1)}, u32[]{:S(2)}, u32[]{:S(2)}) collective-permute-start(f32[1,16,1024]{2,0,1:T(1,128)S(1)} %get-tuple-element.41), channel_id=1, source_target_pairs={{32,0},{64,32},{96,64},{128,96},{160,128},{192,160},{224,192},{33,... | collective-permute-start | bytes 196616 | tf_op jit(solution)/shard_map/ppermute | solution.py:38
  99.7 5.3 collective-permute-start.6
  103.0 5.2 collective-permute-start.7
  276.3 5.0 collective-permute-start.8
  280.0 5.0 collective-permute-start.9
  285.3 6.9 %collective-permute-start.10 = (f32[8,1,1024]{2,0,1:T(8,128)S(1)}, f32[8,1,1024]{2,0,1:T(8,128)S(1)}, u32[]{:S(2)}, u32[]{:S(2)}) collective-permute-start(f32[8,1,1024]{2,0,1:T(8,128)S(1)} %get-tuple-element.34), channel_id=1, source_target_pairs={{0,1},{1,2},{2,3},{3,4},{4,5},{5,6},{6,7},{7,8},{8,9},{9,10},{10,1... | collective-permute-start | bytes 98312 | tf_op jit(solution)/shard_map/ppermute | solution.py:37
  290.3 5.2 collective-permute-start.11
  457.7 5.0 collective-permute-start.12
  461.4 5.0 collective-permute-start.13
  466.7 7.0 %collective-permute-start.14 = (f32[8,1,1024]{2,0,1:T(8,128)S(1)}, f32[8,1,1024]{2,0,1:T(8,128)S(1)}, u32[]{:S(2)}, u32[]{:S(2)}) collective-permute-start(f32[8,1,1024]{2,0,1:T(8,128)S(1)} %get-tuple-element.30), channel_id=1, source_target_pairs={{0,1},{1,2},{2,3},{3,4},{4,5},{5,6},{6,7},{7,8},{8,9},{9,10},{10,1... | collective-permute-start | bytes 98312 | tf_op jit(solution)/shard_map/ppermute | solution.py:37
  471.7 5.2 collective-permute-start.15
